TPU v7x, 256 devices: a whole 4x4x8 slice. The times are simulated.
256 devices in a mesh: gx: 32 (over z, x), gy: 8 (over y, core).
Axes of the slice: x: 4, y: 4, z: 8, core: 2. Of those that a mesh axis runs over, the one named last changes fastest.
Arguments:
- hidden_in: bfloat16 [64, 5120], P(None, 'gx'), may hold values from -60 to 60
- norm1_gain: float32 [5120], P('gx'), may hold values from 0.1 to 1.9
- norm1_bias: float32 [5120], P('gx'), may hold values from -4 to 4
- norm2_gain: float32 [5120], P('gx'), may hold values from 0.1 to 1.9
- norm2_bias: float32 [5120], P('gx'), may hold values from -4 to 4
- w_qkv: bfloat16 [5120, 15360], P('gx', 'gy'), may hold values from -0.078125 to 0.078125
- b_qkv: float32 [15360], P('gy'), may hold values from -4 to 4
- w_out: bfloat16 [5120, 5120], P('gy', 'gx'), may hold values from -0.078125 to 0.078125
- b_out: float32 [5120], P('gx'), may hold values from -4 to 4
- w_up: bfloat16 [5120, 20480], P('gx', 'gy'), may hold values from -0.078125 to 0.078125
- b_up: float32 [20480], P('gy'), may hold values from -4 to 4
- w_down: bfloat16 [20480, 5120], P('gy', 'gx'), may hold values from -0.0390625 to 0.0390625
- b_down: float32 [5120], P('gx'), may hold values from -4 to 4
- key_cache: bfloat16 [64, 40, 1024, 128], P('gx', 'gy'), may hold values from -70 to 70
- value_cache: bfloat16 [64, 40, 1024, 128], P('gx', 'gy'), may hold values from -6 to 6
- lengths: int32 [64], replicated, may hold values from 1 to 1024, 32768 in all
- assignment: int32 [64], replicated, may hold values from 0 to 63, each once
Outputs:
- hidden_out: bfloat16 [64, 5120], P(None, 'gx')
- new_keys: bfloat16 [64, 40, 1024, 128], P('gx', 'gy')
- new_values: bfloat16 [64, 40, 1024, 128], P('gx', 'gy')
Inputs may be any that keep to these rules, and one draw needn't show every extreme that they name: `lengths`: each request's length, the largest exactly 1024. `assignment`: a permutation: every slot holds exactly one request.
All inputs are finite; a program needn't handle non-finite values.
Results may differ from a plain program's by a relative error of at most 0.0068.
Values may be sent and summed in bfloat16 or wider, within the bound.
No kernel may reach another device: no remote copies, remote signals or barrier semaphores. Data moves between devices by JAX's collectives and lax.ppermute only.
A program may use at most 64 MiB of HBM per device.

v0:
```python
import jax
import jax.numpy as jnp
from jax import lax
from jax.sharding import PartitionSpec as P

D = 5120
HD = 128
ROT = 32


def rotate(tensor, position):
    half_rot = ROT // 2
    frequency = 10000.0 ** (-2.0 * jnp.arange(half_rot, dtype=jnp.float32) / ROT)
    angle = position.astype(jnp.float32)[:, None, None] * frequency
    cosine = jnp.cos(angle)
    sine = jnp.sin(angle)
    first_half = tensor[..., :half_rot]
    second_half = tensor[..., half_rot:ROT]
    return jnp.concatenate(
        [
            first_half * cosine - second_half * sine,
            second_half * cosine + first_half * sine,
            tensor[..., ROT:],
        ],
        axis=-1,
    )


def block_scores(query, keys, my_len):
    span_len = keys.shape[2]
    scores = jnp.einsum("shd,shpd->shp", query, keys, preferred_element_type=jnp.float32) * HD ** (
        -0.5
    )
    places = lax.iota(jnp.int32, span_len)
    valid = places[None, None, :] < my_len[:, None, None]
    return (jnp.where(valid, scores, -1e30), valid)


def on_device(
    hidden_in,
    norm1_gain,
    norm1_bias,
    norm2_gain,
    norm2_bias,
    w_qkv,
    b_qkv,
    w_out,
    b_out,
    w_up,
    b_up,
    w_down,
    b_down,
    key_cache,
    value_cache,
    lengths,
    assignment,
):
    requests = hidden_in.shape[0]
    rows_dev = key_cache.shape[0]
    heads_dev = key_cache.shape[1]
    wide_in = hidden_in.astype(jnp.float32)
    sum_rows, sum_squares = lax.psum(
        (jnp.sum(wide_in, axis=1), jnp.sum(wide_in * wide_in, axis=1)), "gx"
    )
    row_mean = sum_rows / D
    row_var = sum_squares / D - row_mean * row_mean
    normed = (wide_in - row_mean[:, None]) * lax.rsqrt(row_var + 1e-05)[:, None]
    attn_in = (normed * norm1_gain + norm1_bias).astype(jnp.bfloat16)
    mlp_in = (normed * norm2_gain + norm2_bias).astype(jnp.bfloat16)
    slot_ids = lax.iota(jnp.int32, requests)
    matches = assignment[:, None] == slot_ids[None, :]
    to_request = matches.astype(jnp.float32)
    attn_slot = jnp.dot(
        matches.T.astype(jnp.bfloat16), attn_in, preferred_element_type=jnp.float32
    ).astype(jnp.bfloat16)
    slot_len = jnp.sum(jnp.where(matches, lengths[:, None], 0), axis=0)
    my_len = lax.dynamic_slice_in_dim(slot_len, lax.axis_index("gx") * rows_dev, rows_dev, 0)
    qkv = (
        lax.psum_scatter(
            jnp.dot(attn_slot, w_qkv, preferred_element_type=jnp.float32),
            "gx",
            scatter_dimension=0,
            tiled=True,
        )
        + b_qkv
    )
    qkv = qkv.reshape(rows_dev, heads_dev, 3, HD)
    position = my_len - 1
    query = rotate(qkv[:, :, 0], position).astype(jnp.bfloat16)
    new_key = rotate(qkv[:, :, 1], position).astype(jnp.bfloat16)
    new_value = qkv[:, :, 2].astype(jnp.bfloat16)
    new_keys = key_cache
    new_values = value_cache
    zero_index = jnp.int32(0)
    for local_slot in range(rows_dev):
        slot_index = jnp.int32(local_slot)
        new_keys = lax.dynamic_update_slice(
            new_keys,
            new_key[local_slot][None, :, None, :],
            (slot_index, zero_index, position[local_slot], zero_index),
        )
        new_values = lax.dynamic_update_slice(
            new_values,
            new_value[local_slot][None, :, None, :],
            (slot_index, zero_index, position[local_slot], zero_index),
        )
    scores, valid = block_scores(query, new_keys, my_len)
    top_score = jnp.max(scores, axis=2)
    weights = jnp.where(valid, jnp.exp(scores - top_score[:, :, None]), 0.0)
    total = jnp.sum(weights, axis=2)
    weights_low = weights.astype(jnp.bfloat16)
    weighted = jnp.einsum(
        "shp,shpd->shd", weights_low, new_values, preferred_element_type=jnp.float32
    )
    attended = (weighted / total[:, :, None]).astype(jnp.bfloat16).reshape(rows_dev, heads_dev * HD)
    slot_part = jnp.dot(
        lax.all_gather(attended, "gx", axis=0, tiled=True),
        w_out,
        preferred_element_type=jnp.float32,
    )
    attn_part = jnp.dot(to_request, slot_part, precision=lax.Precision.HIGHEST)
    up_partial = jnp.dot(mlp_in, w_up, preferred_element_type=jnp.float32)
    up = lax.psum(up_partial, "gx") + b_up
    hidden = jax.nn.gelu(up, approximate=False).astype(jnp.bfloat16)
    mlp_part = jnp.dot(hidden, w_down, preferred_element_type=jnp.float32)
    branches = lax.psum(attn_part + mlp_part, "gy")
    hidden_out = (wide_in + branches + b_out + b_down).astype(jnp.bfloat16)
    return (hidden_out, new_keys, new_values)


def solution(mesh):
    return jax.shard_map(
        on_device,
        mesh=mesh,
        in_specs=(
            P(None, "gx"),
            P("gx"),
            P("gx"),
            P("gx"),
            P("gx"),
            P("gx", "gy"),
            P("gy"),
            P("gy", "gx"),
            P("gx"),
            P("gx", "gy"),
            P("gy"),
            P("gy", "gx"),
            P("gx"),
            P("gx", "gy", None, None),
            P("gx", "gy", None, None),
            P(),
            P(),
        ),
        out_specs=(P(None, "gx"), P("gx", "gy", None, None), P("gx", "gy", None, None)),
        check_vma=False,
    )
```

profile of v0, /device:TPU:2, one launch (start us, length us, event | category | flops | bytes accessed | tf_op | source)
XLA Modules:
  0.0 324.9 jit_solution(3638242814341928627)
XLA Ops:
  7.2 1.8 copy-done.3
  9.0 1.5 copy.66
  10.5 0.1 convert_reduce_fusion
  10.7 73.7 %all-reduce.1 = (f32[64]{0:T(128)S(1)}, f32[64]{0:T(128)S(1)}) all-reduce(f32[64]{0:T(128)S(1)} %get-tuple-element.4, f32[64]{0:T(128)S(1)} %get-tuple-element.3), channel_id=1, replica_groups=mesh['gx'=32,'gy'=8] {'gx'}, use_global_device_ids=true, to_apply=%region_4.5 | all-reduce | flops 128 | bytes 1024 | tf_op jit(solution)/shard_map/psum | solution.py:62
  84.4 1.2 fusion.61
  85.5 2.5 fusion.4
  88.1 0.1 select_reduce_fusion
  88.2 0.1 fusion.118
  88.3 0.6 fusion.122
  91.5 0.6 dynamic-slice
  94.1 0.1 multiply_cosine_fusion
  94.3 142.2 %all-reduce.5.cloned.1.call-done = (f32[64,1920]{1,0:T(8,128)}, f32[64,2560]{1,0:T(8,128)}) async-done(((f32[64,1920]{1,0:T(8,128)}, f32[64,2560]{1,0:T(8,128)}), (f32[64,1920]{1,0:T(8,128)}, f32[64,2560]{1,0:T(8,128)})) %all-reduce.5.cloned.1.call-update) | async-done | bytes 1146896
  236.5 0.8 dynamic-slice_add_fusion
  237.5 0.1 subtract_convert_fusion.1
  237.6 0.1 pad_maximum_fusion
  237.7 1.3 dynamic_update_slice.12
  239.1 0.1 maximum_bitcast_fusion
  239.1 1.3 dynamic_update_slice.13
  240.5 2.5 fusion.84
  243.0 0.1 fusion.3
  243.1 0.1 fusion.119
  243.2 0.1 copy.42
  243.4 0.4 fusion.59
  243.8 0.1 fusion.83
  243.9 0.9 reshape.113
  244.8 41.8 %all-gather = bf16[32,2,640]{2,1,0:T(2,128)(2,1)S(1)} all-gather(bf16[1,2,640]{2,1,0:T(2,128)(2,1)} %reshape.113), channel_id=1, replica_groups=mesh['gx'=32,'gy'=8] {'gx'}, dimensions={0}, use_global_device_ids=true | all-gather | bytes 84480 | tf_op jit(solution)/shard_map/all_gather | solution.py:117
  286.6 0.7 reshape.114
  287.3 1.1 fusion.123
  288.5 0.9 fusion.77
  289.4 3.5 %convolution_add_fusion = f32[64,160]{1,0:T(8,128)} fusion(f32[64,160]{1,0:T(8,128)S(1)} %fusion.77, bf16[2560,160]{0,1:T(8,128)(2,1)} %param.28, f32[64,2560]{1,0:T(8,128)} %get-tuple-element.8, f32[2560]{0:T(1024)} %param.27), kind=kOutput, calls=%fused_computation.1 | convolution fusion | flops 63252480 | bytes 1566720 | tf_op jit(solution)/shard_map/dot_general | solution.py:125
  292.9 24.5 %psum.31 = f32[64,160]{1,0:T(8,128)S(1)} all-reduce(f32[64,160]{1,0:T(8,128)} %convolution_add_fusion), channel_id=1, replica_groups=mesh['gx'=32,'gy'=8] {'gy'}, use_global_device_ids=true, to_apply=%region_9.10 | all-reduce | flops 10240 | bytes 81920 | tf_op jit(solution)/shard_map/psum | solution.py:126
  317.4 0.6 fusion.57
  (45 shorter events, 0.5 us)
Async XLA Ops:
  7.2 77.2 %copy-start = (bf16[160,2560]{1,0:T(8,128)(2,1)S(1)}, bf16[160,2560]{1,0:T(8,128)(2,1)}, u32[]{:S(2)}) copy-start(bf16[160,2560]{1,0:T(8,128)(2,1)} %param.26) | copy-start | bytes 2457604
  7.2 1.8 copy-start.3
  7.2 229.3 %all-reduce.5.cloned.1.call-start = ((), (), s32[]{:S(2)}) async-start(), calls=%async_computation | async-start | bytes 2293760
  9.0 1.5 copy-start.4
  9.0 75.4 %copy-start.7 = (f32[160]{0:T(256)S(1)}, f32[160]{0:T(256)}, u32[]{:S(2)}) copy-start(f32[160]{0:T(256)} %param.21) | copy-start | bytes 1924
  9.0 75.4 %copy-start.8 = (f32[160]{0:T(256)S(1)}, f32[160]{0:T(256)}, u32[]{:S(2)}) copy-start(f32[160]{0:T(256)} %param.20) | copy-start | bytes 1924
  9.0 76.5 %copy-start.6 = (s32[64]{0:T(128)S(1)}, s32[64]{0:T(128)}, u32[]{:S(2)}) copy-start(s32[64]{0:T(128)} %param.33) | copy-start | bytes 772
  9.0 76.5 %copy-start.9 = (f32[160]{0:T(256)S(1)}, f32[160]{0:T(256)}, u32[]{:S(2)}) copy-start(f32[160]{0:T(256)} %param.19) | copy-start | bytes 1924
  9.0 76.5 %copy-start.10 = (f32[160]{0:T(256)S(1)}, f32[160]{0:T(256)}, u32[]{:S(2)}) copy-start(f32[160]{0:T(256)} %param.18) | copy-start | bytes 1924
  10.5 77.6 %copy-start.13 = (s32[64]{0:T(128)S(1)}, s32[64]{0:T(128)}, u32[]{:S(2)}) copy-start(s32[64]{0:T(128)} %param.32) | copy-start | bytes 772
  10.5 81.0 %copy-start.14 = (u32[256]{0:T(256)S(1)}, u32[256]{0:T(256)}, u32[]{:S(2)}) copy-start(u32[256]{0:T(256)} %constant.103) | copy-start | bytes 3076
  10.5 225.9 %copy-start.5 = (f32[1920]{0:T(1024)S(1)}, f32[1920]{0:T(1024)}, u32[]{:S(2)}) copy-start(f32[1920]{0:T(1024)} %param.23) | copy-start | bytes 23044
  85.5 157.8 %copy-start.2 = (bf16[2,5,1024,128]{3,2,1,0:T(8,128)(2,1)S(1)}, bf16[2,5,1024,128]{3,2,1,0:T(8,128)(2,1)}, u32[]{:S(2)}) copy-start(bf16[2,5,1024,128]{3,2,1,0:T(8,128)(2,1)} %param.31) | copy-start | bytes 7864324
  243.4 49.5 %copy-start.1 = (bf16[2,5,1024,128]{3,2,1,0:T(8,128)(2,1)}, bf16[2,5,1024,128]{3,2,1,0:T(8,128)(2,1)S(1)}, u32[]{:S(2)}) copy-start(bf16[2,5,1024,128]{3,2,1,0:T(8,128)(2,1)S(1)} %dynamic_update_slice.15) | copy-start | bytes 7864324
  289.3 28.1 %copy-start.11 = (f32[160]{0:T(256)S(1)}, f32[160]{0:T(256)}, u32[]{:S(2)}) copy-start(f32[160]{0:T(256)} %param.29) | copy-start | bytes 1924
  289.4 28.1 %copy-start.12 = (f32[160]{0:T(256)S(1)}, f32[160]{0:T(256)}, u32[]{:S(2)}) copy-start(f32[160]{0:T(256)} %param.25) | copy-start | bytes 1924
Sparse Core Ops, SparseCore 0:
  88.2 148.2 all-reduce.4
where the time goes:
time: 325 us
  waiting for transfers between devices  142 us (44%)
  blocking collectives  140 us (43%)
  between operations  18.9 us (6%)
  matrix products  12.2 us (4%)
  local copies, waits for them, and re-layouts  9.11 us (3%)
    unnamed x2, waiting for transfers between devices  142 us
    psum x1, blocking collectives, on_device(): lax.psum((jnp.sum(wide_in, axis=1), jnp.sum(wide_in * wide_in, axis=1)),...  73.7 us
    all_gather x1, blocking collectives, on_device(): lax.all_gather(attended, 'gx', axis=0, tiled=True)  41.8 us
    psum x1, blocking collectives, on_device(): branches = lax.psum(attn_part + mlp_part, 'gy')  24.5 us
  transfers between devices with their start and end apart: 1, of which 1 were waited for; matrix products, arithmetic and copies ran while one was open for 0% of the time, Pallas kernels for 0%

commit v1 on v0

--- a/solution.py
+++ b/solution.py
@@ -114,7 +114,9 @@
     )
     attended = (weighted / total[:, :, None]).astype(jnp.bfloat16).reshape(rows_dev, heads_dev * HD)
     slot_part = jnp.dot(
-        lax.all_gather(attended, "gx", axis=0, tiled=True),
+        jnp.concatenate(
+            lax.all_to_all(jnp.stack([attended] * lax.axis_size("gx")), "gx", 0, 0), axis=0
+        ),
         w_out,
         preferred_element_type=jnp.float32,
     )

time: 325 us -> 299 us (0.920)
  blocking collectives: 140 us -> 114 us
    all_gather x1 -> x0, blocking collectives: 41.8 us -> none  [on_device(): lax.all_gather(attended, 'gx', axis=0, tiled=True)]
    all_to_all x0 -> x1, blocking collectives: none -> 16 us  [on_device(): lax.all_to_all(jnp.stack([attended] * lax.axis_size('gx')), 'gx', 0, 0)]
  transfers between devices with their start and end apart: 1 -> 1, of which waited for: 1 -> 1; matrix products, arithmetic and copies ran while one was open for 0% -> 1% of each run, Pallas kernels for 0% -> 0%
where the time goes in v1:
time: 299 us; the launch traced here: 298 us
  waiting for transfers between devices  142 us (47%)
  blocking collectives  114 us (38%)
  between operations  18.9 us (6%)
  matrix products  12.2 us (4%)
  local copies, waits for them, and re-layouts  8.26 us (3%)
    unnamed x2, waiting for transfers between devices  142 us
    psum x1, blocking collectives, on_device(): lax.psum((jnp.sum(wide_in, axis=1), jnp.sum(wide_in * wide_in, axis=1)),...  73.7 us
    psum x1, blocking collectives, on_device(): branches = lax.psum(attn_part + mlp_part, 'gy')  24.5 us
    all_to_all x1, blocking collectives, on_device(): lax.all_to_all(jnp.stack([attended] * lax.axis_size('gx')), 'gx', 0, 0)  16 us
  transfers between devices with their start and end apart: 1, of which 1 were waited for; matrix products, arithmetic and copies ran while one was open for 1% of the time, Pallas kernels for 0%

profile of v1, /device:TPU:2, one launch (start us, length us, event | category | flops | bytes accessed | tf_op | source)
XLA Modules:
  0.0 298.2 jit_solution(8507129718702844701)
XLA Ops:
  7.2 1.8 copy-done.3
  9.0 1.5 copy.71
  10.5 0.1 convert_reduce_fusion
  10.7 73.7 %all-reduce.1 = (f32[64]{0:T(128)S(1)}, f32[64]{0:T(128)S(1)}) all-reduce(f32[64]{0:T(128)S(1)} %get-tuple-element.4, f32[64]{0:T(128)S(1)} %get-tuple-element.3), channel_id=1, replica_groups=mesh['gx'=32,'gy'=8] {'gx'}, use_global_device_ids=true, to_apply=%region_4.5 | all-reduce | flops 128 | bytes 1024 | tf_op jit(solution)/shard_map/psum | solution.py:62
  84.4 1.2 fusion.61
  85.5 2.5 fusion.4
  88.1 0.1 select_reduce_fusion
  88.2 0.1 broadcast_add_fusion
  88.3 0.6 fusion.122
  91.5 0.6 dynamic-slice
  94.1 0.1 multiply_cosine_fusion
  94.3 142.2 %all-reduce.5.cloned.1.call-done = (f32[64,1920]{1,0:T(8,128)}, f32[64,2560]{1,0:T(8,128)}) async-done(((f32[64,1920]{1,0:T(8,128)}, f32[64,2560]{1,0:T(8,128)}), (f32[64,1920]{1,0:T(8,128)}, f32[64,2560]{1,0:T(8,128)})) %all-reduce.5.cloned.1.call-update) | async-done | bytes 1146896
  236.5 0.8 dynamic-slice_add_fusion
  237.4 0.1 slice.91
  237.5 0.1 subtract_convert_fusion.1
  237.6 0.1 pad_maximum_fusion
  237.7 0.1 maximum_bitcast_fusion
  237.8 1.3 dynamic_update_slice.12
  239.1 1.3 dynamic_update_slice.13
  240.5 2.5 fusion.84
  243.0 0.1 fusion.3
  243.1 0.1 convert_bitcast_fusion
  243.2 0.1 copy.42
  243.4 0.4 fusion.59
  243.8 0.1 fusion.86
  244.0 16.0 %all_to_all.5 = bf16[32,2,640]{2,1,0:T(2,128)(2,1)S(1)} all-to-all(bf16[32,2,640]{2,1,0:T(2,128)(2,1)S(1)} %stack.3), channel_id=1, replica_groups=mesh['gx'=32,'gy'=8] {'gx'}, dimensions={0} | all-to-all | bytes 163840 | tf_op jit(solution)/shard_map/all_to_all | solution.py:118
  259.9 0.7 reshape.114
  260.6 1.2 fusion.123
  261.8 0.9 fusion.77
  262.7 3.5 %convolution_add_fusion = f32[64,160]{1,0:T(8,128)} fusion(f32[64,160]{1,0:T(8,128)S(1)} %fusion.77, bf16[2560,160]{0,1:T(8,128)(2,1)} %param.28, f32[64,2560]{1,0:T(8,128)} %get-tuple-element.8, f32[2560]{0:T(1024)} %param.27), kind=kOutput, calls=%fused_computation.1 | convolution fusion | flops 63252480 | bytes 1566720 | tf_op jit(solution)/shard_map/dot_general | solution.py:127
  266.3 24.5 %psum.31 = f32[64,160]{1,0:T(8,128)S(1)} all-reduce(f32[64,160]{1,0:T(8,128)} %convolution_add_fusion), channel_id=1, replica_groups=mesh['gx'=32,'gy'=8] {'gy'}, use_global_device_ids=true, to_apply=%region_9.10 | all-reduce | flops 10240 | bytes 81920 | tf_op jit(solution)/shard_map/psum | solution.py:128
  290.8 0.6 fusion.57
  (46 shorter events, 0.5 us)
Async XLA Ops:
  7.2 77.2 %copy-start = (bf16[160,2560]{1,0:T(8,128)(2,1)S(1)}, bf16[160,2560]{1,0:T(8,128)(2,1)}, u32[]{:S(2)}) copy-start(bf16[160,2560]{1,0:T(8,128)(2,1)} %param.26) | copy-start | bytes 2457604
  7.2 1.8 copy-start.3
  7.2 229.3 %all-reduce.5.cloned.1.call-start = ((), (), s32[]{:S(2)}) async-start(), calls=%async_computation.1 | async-start | bytes 2293760
  9.0 1.5 copy-start.4
  9.0 75.4 %copy-start.7 = (f32[160]{0:T(256)S(1)}, f32[160]{0:T(256)}, u32[]{:S(2)}) copy-start(f32[160]{0:T(256)} %param.21) | copy-start | bytes 1924
  9.0 75.4 %copy-start.8 = (f32[160]{0:T(256)S(1)}, f32[160]{0:T(256)}, u32[]{:S(2)}) copy-start(f32[160]{0:T(256)} %param.20) | copy-start | bytes 1924
  9.0 76.5 %copy-start.6 = (s32[64]{0:T(128)S(1)}, s32[64]{0:T(128)}, u32[]{:S(2)}) copy-start(s32[64]{0:T(128)} %param.33) | copy-start | bytes 772
  9.0 76.5 %copy-start.9 = (f32[160]{0:T(256)S(1)}, f32[160]{0:T(256)}, u32[]{:S(2)}) copy-start(f32[160]{0:T(256)} %param.19) | copy-start | bytes 1924
  9.0 76.5 %copy-start.10 = (f32[160]{0:T(256)S(1)}, f32[160]{0:T(256)}, u32[]{:S(2)}) copy-start(f32[160]{0:T(256)} %param.18) | copy-start | bytes 1924
  10.5 77.6 %copy-start.13 = (s32[64]{0:T(128)S(1)}, s32[64]{0:T(128)}, u32[]{:S(2)}) copy-start(s32[64]{0:T(128)} %param.32) | copy-start | bytes 772
  10.5 81.0 %copy-start.14 = (u32[256]{0:T(256)S(1)}, u32[256]{0:T(256)}, u32[]{:S(2)}) copy-start(u32[256]{0:T(256)} %constant.103) | copy-start | bytes 3076
  10.5 225.9 %copy-start.5 = (f32[1920]{0:T(1024)S(1)}, f32[1920]{0:T(1024)}, u32[]{:S(2)}) copy-start(f32[1920]{0:T(1024)} %param.23) | copy-start | bytes 23044
  85.5 157.8 %copy-start.2 = (bf16[2,5,1024,128]{3,2,1,0:T(8,128)(2,1)S(1)}, bf16[2,5,1024,128]{3,2,1,0:T(8,128)(2,1)}, u32[]{:S(2)}) copy-start(bf16[2,5,1024,128]{3,2,1,0:T(8,128)(2,1)} %param.31) | copy-start | bytes 7864324
  243.4 22.9 %copy-start.1 = (bf16[2,5,1024,128]{3,2,1,0:T(8,128)(2,1)}, bf16[2,5,1024,128]{3,2,1,0:T(8,128)(2,1)S(1)}, u32[]{:S(2)}) copy-start(bf16[2,5,1024,128]{3,2,1,0:T(8,128)(2,1)S(1)} %dynamic_update_slice.15) | copy-start | bytes 7864324
  262.7 28.1 %copy-start.11 = (f32[160]{0:T(256)S(1)}, f32[160]{0:T(256)}, u32[]{:S(2)}) copy-start(f32[160]{0:T(256)} %param.29) | copy-start | bytes 1924
  262.7 28.1 %copy-start.12 = (f32[160]{0:T(256)S(1)}, f32[160]{0:T(256)}, u32[]{:S(2)}) copy-start(f32[160]{0:T(256)} %param.25) | copy-start | bytes 1924
Sparse Core Ops, SparseCore 0:
  88.2 148.2 all-reduce.4
